TPU v7x, 32 devices: a whole 2x2x4 slice. The times are simulated.
32 devices in a mesh: days: 2 (over y), chan: 4 (over z), win: 4 (over x, core).
Axes of the slice: x: 2, y: 2, z: 4, core: 2. Of those that a mesh axis runs over, the one named last changes fastest.
Arguments:
- spectra: bfloat16 [2560, 32, 1024], P(('days', 'chan'), 'win'), parts along dimension 0, may hold values from -17 to 17
- pair_anchor: int32 [2048], P('chan'), may hold values from 0 to 319
- pair_offset: int32 [2048], P('chan'), may hold values from 0 to 2
- pair_partner: int32 [2048], P('chan'), may hold values from 0 to 319
- pair_count: int32 [4], P('chan'), may hold values from 1 to 512, as said below
- window_bins: int32 [64], P(('days', 'win')), parts along dimension 0, may hold values from 0 to 7
- bin_gain: float32 [8], replicated, may hold values from 0.2 to 5
Outputs:
- ref_stack: float32 [4096, 128], P(('days', 'chan')), parts along dimension 0
- restack: float32 [4096, 128], P(('days', 'chan')), parts along dimension 0
There are 2 independent parts, one for each index of `days`. A program takes and returns all parts, laid end to end along the dimension named above; an argument that names none is the same for every part. Nothing has to cross between parts.
Inputs may be any that keep to these rules, and one draw needn't show every extreme that they name: `pair_count`: each block holds from 1 to 512 live pair slots, the first ones of its slots; some block holds 512 in every draw.
All inputs are finite; a program needn't handle non-finite values.
Results may differ from a plain program's by a relative error of at most 0.0062.
Values may be sent and summed in bfloat16 or wider, within the bound.
No kernel may reach another device: no remote copies, remote signals or barrier semaphores. Data moves between devices by JAX's collectives and lax.ppermute only.
A program may use at most 128 MiB of HBM per device.

v0:
```python
import jax
import jax.numpy as jnp
from jax import lax
from jax.experimental import pallas as pl
from jax.experimental.pallas import tpu as pltpu
from jax.sharding import PartitionSpec as P

LAG = 128


EPS_POWER = 1e-05
EPS_LAG = 1e-06


def whiten(spectra):
    spectra_f = spectra.astype(jnp.float32)
    power_mean = jnp.mean(spectra_f * spectra_f, axis=-1, keepdims=True)
    return (spectra_f * lax.rsqrt(power_mean + EPS_POWER)).astype(jnp.bfloat16)


def lag_table(freq_count, lag_count):
    freq_ids = lax.broadcasted_iota(jnp.float32, (freq_count, lag_count), 0)
    lag_ids = lax.broadcasted_iota(jnp.float32, (freq_count, lag_count), 1) - lag_count // 2
    angles = 2.0 * jnp.pi / (2 * freq_count) * freq_ids * lag_ids
    norm_scale = 1.0 / jnp.sqrt(jnp.float32(freq_count))
    return jnp.concatenate(
        [jnp.cos(angles) * norm_scale, -jnp.sin(angles) * norm_scale], axis=0
    ).astype(jnp.bfloat16)


def cross_spectra(anchors, partners):
    half_width = anchors.shape[-1] // 2
    anchor_f = anchors.astype(jnp.float32)
    partner_f = partners.astype(jnp.float32)
    anchor_re = anchor_f[..., :half_width]
    anchor_im = anchor_f[..., half_width:]
    partner_re = partner_f[..., :half_width]
    partner_im = partner_f[..., half_width:]
    cross_re = anchor_re * partner_re + anchor_im * partner_im
    cross_im = anchor_im * partner_re - anchor_re * partner_im
    return jnp.concatenate([cross_re, cross_im], axis=-1).astype(jnp.bfloat16)


def window_gains(bins, gains):
    levels = lax.broadcasted_iota(jnp.int32, (bins.shape[0], gains.shape[0]), 1)
    return jnp.sum(jnp.where(bins[:, None] == levels, gains[None, :], jnp.float32(0.0)), axis=1)


def window_weights(lag_corr, ref_sum, window_gain):
    corr_f = lag_corr.astype(jnp.float32)
    inner_prod = jnp.mean(corr_f * ref_sum[:, None, :], axis=-1)
    corr_rms = jnp.sqrt(jnp.mean(corr_f * corr_f, axis=-1) + EPS_LAG)
    ref_rms = jnp.sqrt(jnp.mean(ref_sum * ref_sum, axis=-1) + EPS_LAG)
    coherence = inner_prod / (corr_rms * ref_rms[:, None])
    weights = window_gain[None, :] * jnp.exp(2.0 * coherence)
    numerator = jnp.sum(weights[:, :, None] * corr_f, axis=1)
    denominator = jnp.sum(weights, axis=1)
    return (numerator, denominator)


def select_rows(selector, rows):
    return jnp.einsum("sc,cwf->swf", selector, rows, preferred_element_type=jnp.bfloat16)


def butterfly_sum(value, axis):
    peers = lax.axis_size(axis)
    if peers & (peers - 1):
        return lax.psum(value, axis)
    step = 1
    while step < peers:
        pairs = [(i, i ^ step) for i in range(peers)]
        value = jax.tree.map(jnp.add, value, lax.ppermute(value, axis, pairs))
        step *= 2
    return value


def ring_exchange(up_rows, down_rows, axis):
    peers = lax.axis_size(axis)
    up = [(i, (i + 1) % peers) for i in range(peers)]
    down = [(j, i) for i, j in up]
    return lax.ppermute(up_rows, axis, up), lax.ppermute(down_rows, axis, down)


def gather_blocks(row, axis):
    peers = lax.axis_size(axis)
    if peers & (peers - 1):
        return lax.all_gather(row, axis)
    me = lax.axis_index(axis)
    acc = row[None]
    step = 1
    while step < peers:
        pairs = [(i, i ^ step) for i in range(peers)]
        got = lax.ppermute(acc, axis, pairs)
        acc = jnp.where((me & step) == 0, jnp.concatenate([acc, got]), jnp.concatenate([got, acc]))
        step *= 2
    return acc


def onehot(index, size, mask):
    return (index[:, None] == lax.broadcasted_iota(jnp.int32, (index.shape[0], size), 1)) & mask[:, None]


def window_weights_wm(corr_f, ref_sum, window_gain):
    inner_prod = jnp.mean(corr_f * ref_sum[None, :, :], axis=-1)
    corr_rms = jnp.sqrt(jnp.mean(corr_f * corr_f, axis=-1) + EPS_LAG)
    ref_rms = jnp.sqrt(jnp.mean(ref_sum * ref_sum, axis=-1) + EPS_LAG)
    coherence = inner_prod / (corr_rms * ref_rms[None, :])
    weights = window_gain[:, None] * jnp.exp(2.0 * coherence)
    numerator = jnp.sum(weights[:, :, None] * corr_f, axis=0)
    denominator = jnp.sum(weights, axis=0)
    return (numerator, denominator)


def block_needs(offs, parts, count, block_chans):
    live = lax.broadcasted_iota(jnp.int32, offs.shape, 0) < count
    hit = parts[:, None] == lax.broadcasted_iota(jnp.int32, (1, block_chans), 1)
    need_minus = jnp.any(hit & (live & (offs == 0))[:, None], axis=0)
    need_plus = jnp.any(hit & (live & (offs == 2))[:, None], axis=0)
    pos_minus = jnp.cumsum(need_minus, dtype=jnp.int32) - 1
    pos_plus = jnp.cumsum(need_plus, dtype=jnp.int32) - 1
    return need_minus, need_plus, pos_minus, pos_plus


def cross_kernel(anchor_ref, own_ref, sbf_ref, saf_ref, bf_ref, af_ref, t_ref, corr_ref):
    wins = anchor_ref.shape[0]
    half = anchor_ref.shape[2] // 2
    t_re = t_ref[:half, :]
    t_im = t_ref[half:, :]
    sbf, saf = sbf_ref[...], saf_ref[...]
    for w in range(wins):
        part = (
            own_ref[w].astype(jnp.float32)
            + jnp.dot(sbf, bf_ref[w], preferred_element_type=jnp.float32)
            + jnp.dot(saf, af_ref[w], preferred_element_type=jnp.float32)
        )
        anc = anchor_ref[w].astype(jnp.float32)
        a_re, a_im = anc[:, :half], anc[:, half:]
        p_re, p_im = part[:, :half], part[:, half:]
        c_re = (a_re * p_re + a_im * p_im).astype(jnp.bfloat16)
        c_im = (a_im * p_re - a_re * p_im).astype(jnp.bfloat16)
        corr_ref[w] = jnp.dot(c_re, t_re, preferred_element_type=jnp.float32) + jnp.dot(
            c_im, t_im, preferred_element_type=jnp.float32
        )


def halo_cross(chunk, wins, anchors, own, sels, bufs, transform):
    _, slots, width = anchors.shape
    lag_count = transform.shape[1]
    group = min(256, slots)
    row_spec = pl.BlockSpec((wins, group, width), lambda i: (chunk, i, 0))
    sel_specs = [pl.BlockSpec((group, sel.shape[1]), lambda i: (i, 0)) for sel in sels]
    buf_specs = [pl.BlockSpec((wins,) + buf.shape[1:], lambda i: (0, 0, 0)) for buf in bufs]
    return pl.pallas_call(
        cross_kernel,
        grid=(slots // group,),
        in_specs=[row_spec, row_spec] + sel_specs + buf_specs + [pl.BlockSpec(transform.shape, lambda i: (0, 0))],
        out_specs=pl.BlockSpec((wins, group, lag_count), lambda i: (0, i, 0)),
        out_shape=jax.ShapeDtypeStruct((wins, slots, lag_count), jnp.float32),
        compiler_params=pltpu.CompilerParams(vmem_limit_bytes=56 * 1024 * 1024),
    )(anchors, own, *sels, *bufs, transform)


def local(spectra, pair_anchor, pair_offset, pair_partner, pair_count, window_bins, bin_gain):
    block_chans, local_wins, spec_width = spectra.shape
    pair_slots = pair_anchor.shape[0]
    fast_rows = (block_chans // 2 + 15) // 16 * 16
    spill_rows = block_chans - fast_rows

    blocks = lax.axis_size("chan")
    block = lax.axis_index("chan")
    table = jnp.concatenate([pair_offset, pair_partner, pair_count])
    tables = gather_blocks(table, "chan")
    table_before = tables[(block + blocks - 1) % blocks]
    table_after = tables[(block + 1) % blocks]

    def needs_of(tab):
        return block_needs(tab[:pair_slots], tab[pair_slots:2 * pair_slots], tab[2 * pair_slots], block_chans)

    own_minus, own_plus, own_pos_minus, own_pos_plus = needs_of(table)
    up_need, _, up_pos, _ = needs_of(table_after)
    _, down_need, _, down_pos = needs_of(table_before)
    all_needs = jax.vmap(needs_of)(tables)
    need_most = jnp.maximum(
        jnp.max(jnp.sum(all_needs[0], axis=1, dtype=jnp.int32)),
        jnp.max(jnp.sum(all_needs[1], axis=1, dtype=jnp.int32)),
    )

    def send_selector(need, pos, first, rows):
        return onehot(pos - first, rows, need).T.astype(jnp.bfloat16)

    def gather_rows(first, rows, source, whitened=False):
        up_rows = jnp.einsum("jc,cwf->wjf", send_selector(up_need, up_pos, first, rows), source,
                             preferred_element_type=jnp.bfloat16)
        down_rows = jnp.einsum("jc,cwf->wjf", send_selector(down_need, down_pos, first, rows), source,
                               preferred_element_type=jnp.bfloat16)
        if not whitened:
            up_rows, down_rows = whiten(up_rows), whiten(down_rows)
        return ring_exchange(up_rows, down_rows, "chan"), (up_rows, down_rows)

    chunks = 2 if local_wins % 2 == 0 else 1
    chunk_wins = local_wins // chunks
    fast_sent = [gather_rows(0, fast_rows, spectra[:, c * chunk_wins:(c + 1) * chunk_wins]) for c in range(chunks)]
    fast = [got for got, _ in fast_sent]
    spectra_late, _ = lax.optimization_barrier((spectra, [sent for _, sent in fast_sent]))
    white = whiten(spectra_late)
    spill = need_most > fast_rows

    transform = lag_table(spec_width // 2, LAG)
    lag_count = transform.shape[1]
    live_count = pair_count[0]
    slot_ids = lax.broadcasted_iota(jnp.int32, (pair_slots,), 0)
    live = slot_ids < live_count

    def pick(selector, rows):
        return jnp.einsum("sc,cwf->wsf", selector.astype(jnp.bfloat16), rows, preferred_element_type=jnp.bfloat16)

    anchors = pick(onehot(pair_anchor, block_chans, live), white)
    own = pick(onehot(pair_partner, block_chans, live & (pair_offset == 1)), white)
    own_hit = onehot(pair_partner, block_chans, live)
    before_row = jnp.sum(jnp.where(own_hit, own_pos_minus[None, :], 0), axis=1)
    after_row = jnp.sum(jnp.where(own_hit, own_pos_plus[None, :], 0), axis=1)
    use_before = live & (pair_offset == 0)
    use_after = live & (pair_offset == 2)
    sels = [
        onehot(before_row, fast_rows, use_before).astype(jnp.bfloat16),
        onehot(after_row, fast_rows, use_after).astype(jnp.bfloat16),
    ]
    corr_full = jnp.concatenate([
        halo_cross(c, chunk_wins, anchors, own, sels, [fast[c][0], fast[c][1]], transform)
        for c in range(chunks)
    ])

    def spill_extra(_):
        (got_before, got_after), _ = gather_rows(fast_rows, spill_rows, white, whitened=True)
        spill_sels = [
            onehot(before_row - fast_rows, spill_rows, use_before).astype(jnp.bfloat16),
            onehot(after_row - fast_rows, spill_rows, use_after).astype(jnp.bfloat16),
        ]
        zero_own = jnp.zeros_like(own)
        extra = jnp.concatenate([
            halo_cross(c, chunk_wins, anchors, zero_own, spill_sels,
                       [got_before[c * chunk_wins:(c + 1) * chunk_wins], got_after[c * chunk_wins:(c + 1) * chunk_wins]],
                       transform)
            for c in range(chunks)
        ])
        return extra

    def no_extra(_):
        return jnp.zeros((local_wins, pair_slots, lag_count), jnp.float32)

    spill_late, _ = lax.optimization_barrier((spill, fast[0]))
    corr_full = corr_full + lax.cond(spill_late, spill_extra, no_extra, 0)
    corr_all = lax.reduce_precision(corr_full, exponent_bits=8, mantissa_bits=7)
    running = jnp.sum(corr_full, axis=0)

    ref_sum = butterfly_sum(running, "win")
    norm_scale = jnp.sqrt(jnp.float32(local_wins * lax.axis_size("win")))
    ref_stack = jnp.where(live[:, None], ref_sum / norm_scale, 0.0)
    window_gain = window_gains(window_bins, bin_gain)
    numerator, denominator = window_weights_wm(corr_all, ref_sum, window_gain)
    numerator, denominator = butterfly_sum((numerator, denominator), "win")
    restack = jnp.where(live[:, None], norm_scale * numerator / denominator[:, None], 0.0)
    return (ref_stack, restack)


def solution(mesh):
    in_specs = (
        P(("days", "chan"), "win", None),
        P("chan"),
        P("chan"),
        P("chan"),
        P("chan"),
        P(("days", "win")),
        P(),
    )
    out_specs = (P(("days", "chan"), None), P(("days", "chan"), None))
    return jax.shard_map(local, mesh=mesh, in_specs=in_specs, out_specs=out_specs, check_vma=False)
```

profile of v0, /device:TPU:0, one launch (start us, length us, event | category | flops | bytes accessed | tf_op | source)
XLA Modules:
  0.0 185.7 jit_solution(15250054183920938477)
XLA Ops:
  1.3 0.7 pad_add_fusion
  2.0 3.1 %collective-permute-start.2 = (s32[1,1025]{1,0:T(1,128)S(1)}, s32[1,1025]{1,0:T(1,128)S(1)}, u32[]{:S(2)}, u32[]{:S(2)}) collective-permute-start(s32[1,1025]{1,0:T(1,128)S(1)} %broadcast_in_dim.41), channel_id=1, source_target_pairs={{0,4},{4,0},{8,12},{12,8},{1,5},{5,1},{9,13},{13,9},{2,6},{6,2},{1... | collective-permute-start | bytes 12308 | tf_op jit(solution)/shard_map/ppermute | solution.py:93
  5.1 8.2 %fusion.88 = (bf16[320,4,1024]{2,1,0:T(4,128)(2,1)}, bf16[320,4,1024]{2,1,0:T(4,128)(2,1)S(1)}) fusion(bf16[320,8,1024]{2,1,0:T(8,128)(2,1)} %param.9), kind=kLoop, calls=%fused_computation.166 | loop fusion | bytes 10485760 | tf_op jit(solution)/shard_map/slice | solution.py:202
  13.3 0.2 fusion.50
  13.6 0.3 reduce-window.50
  14.0 0.1 slice_reduce_fusion.1
  14.2 0.3 reduce-window.48
  14.6 0.1 slice_reduce_fusion.2
  14.8 0.2 select_reduce_fusion
  15.0 1.1 fusion.52
  16.2 1.3 fusion.60
  17.5 2.7 %collective-permute-start.3 = (s32[2,1025]{1,0:T(2,128)S(1)}, s32[2,1025]{1,0:T(2,128)S(1)}, u32[]{:S(2)}, u32[]{:S(2)}) collective-permute-start(s32[2,1025]{1,0:T(2,128)S(1)} %add_select_fusion.1), channel_id=1, source_target_pairs={{0,8},{4,12},{8,0},{12,4},{1,9},{5,13},{9,1},{13,5},{2,10},{6,14},... | collective-permute-start | bytes 24608 | tf_op jit(solution)/shard_map/ppermute | solution.py:93
  20.2 1.9 %collective-permute-done.3 = s32[2,1025]{1,0:T(2,128)S(1)} collective-permute-done((s32[2,1025]{1,0:T(2,128)S(1)}, s32[2,1025]{1,0:T(2,128)S(1)}, u32[]{:S(2)}, u32[]{:S(2)}) %collective-permute-start.3) | collective-permute-done | bytes 8232 | tf_op jit(solution)/shard_map/ppermute | solution.py:93
  22.2 0.7 fusion.89
  22.9 0.1 fusion.90
  23.0 1.3 fusion.82
  24.2 0.2 fusion.43
  24.4 0.3 reduce-window.36
  24.8 0.1 slice_reduce_fusion.3
  25.0 0.2 fusion.41
  25.2 0.3 reduce-window.34
  25.7 0.1 slice_reduce_fusion.4
  25.9 3.8 %fusion.16 = (f32[4,160]{1,0:T(4,128)S(1)}, bf16[160,4,1024]{2,0,1:T(8,128)(2,1)S(1)}) fusion(bf16[320,4,1024]{2,1,0:T(4,128)(2,1)} %get-tuple-element.64, s32[320]{0:T(512)S(1)} %slice_add_fusion.2, pred[320]{0:T(512)(128)(4,1)S(1)} %fusion.43), kind=kOutput, calls=%fused_computation.31 | convolution fusion | flops 421498240 | bytes 3936320 | tf_op jit(solution)/shard_map/jc,cwf->wjf/dot_general | solution.py:194
  29.7 2.0 %fusion.18 = (f32[4,160]{1,0:T(4,128)S(1)}, bf16[160,4,1024]{2,0,1:T(8,128)(2,1)S(1)}) fusion(bf16[320,4,1024]{2,1,0:T(4,128)(2,1)S(1)} %copy-done.3, s32[320]{0:T(512)S(1)} %slice_add_fusion.3, pred[320]{0:T(512)(128)(4,1)S(1)} %fusion.41), kind=kOutput, calls=%fused_computation.35 | convolution fusion | flops 421498240 | bytes 3936320 | tf_op jit(solution)/shard_map/jc,cwf->wjf/dot_general | solution.py:192
  31.7 2.0 %fusion.20 = (f32[4,160]{1,0:T(4,128)S(1)}, bf16[160,4,1024]{2,0,1:T(8,128)(2,1)S(1)}) fusion(bf16[320,4,1024]{2,1,0:T(4,128)(2,1)S(1)} %get-tuple-element.65, s32[320]{0:T(512)S(1)} %slice_add_fusion.2, pred[320]{0:T(512)(128)(4,1)S(1)} %fusion.43), kind=kOutput, calls=%fused_computation.39 | convolution fusion | flops 421498240 | bytes 3936320 | tf_op jit(solution)/shard_map/jc,cwf->wjf/dot_general | solution.py:194
  33.6 2.0 %fusion.22 = (f32[4,160]{1,0:T(4,128)S(1)}, bf16[160,4,1024]{2,0,1:T(8,128)(2,1)S(1)}) fusion(bf16[320,4,1024]{2,1,0:T(4,128)(2,1)S(1)} %get-tuple-element.65, s32[320]{0:T(512)S(1)} %slice_add_fusion.3, pred[320]{0:T(512)(128)(4,1)S(1)} %fusion.41), kind=kOutput, calls=%fused_computation.43 | convolution fusion | flops 421498240 | bytes 3936320 | tf_op jit(solution)/shard_map/jc,cwf->wjf/dot_general | solution.py:192
  35.6 0.3 fusion.21
  35.9 2.5 %collective-permute-start.5 = (bf16[4,160,1024]{2,1,0:T(8,128)(2,1)S(1)}, bf16[4,160,1024]{2,1,0:T(8,128)(2,1)}, u32[]{:S(2)}, u32[]{:S(2)}) collective-permute-start(bf16[4,160,1024]{2,1,0:T(8,128)(2,1)S(1)} %fusion.21), channel_id=1, source_target_pairs={{4,0},{8,4},{12,8},{0,12},{5,1},{9,5},{13,9},{1,13},{6,2},{10,6},{... | collective-permute-start | bytes 3932168 | tf_op jit(solution)/shard_map/ppermute | solution.py:81
  38.4 0.3 fusion.23
  38.8 1.4 fusion.17
  40.2 3.8 %collective-permute-start.7 = (bf16[4,160,1024]{2,1,0:T(8,128)(2,1)}, bf16[4,160,1024]{2,1,0:T(8,128)(2,1)}, u32[]{:S(2)}, u32[]{:S(2)}) collective-permute-start(bf16[4,160,1024]{2,1,0:T(8,128)(2,1)} %fusion.17), channel_id=1, source_target_pairs={{4,0},{8,4},{12,8},{0,12},{5,1},{9,5},{13,9},{1,13},{6,2},{10,6},{... | collective-permute-start | bytes 3932168 | tf_op jit(solution)/shard_map/ppermute | solution.py:81
  44.0 1.4 fusion.19
  45.4 0.4 collective-permute-start.6
  45.8 0.1 slice_reduce_fusion
  45.9 5.5 %fusion.14 = f32[320,8]{0,1:T(8,128)S(1)} fusion(bf16[320,8,1024]{2,1,0:T(8,128)(2,1)S(1)} %bitcast.92), kind=kLoop, calls=%fused_computation.25 | loop fusion | flops 7861760 | bytes 5253120 | tf_op jit(solution)/shard_map/reduce_sum | solution.py:17
  51.4 6.5 %fusion.15 = bf16[320,8,1024]{2,0,1:T(8,128)(2,1)} fusion(f32[320,8]{0,1:T(8,128)S(1)} %add_rsqrt_fusion, bf16[320,8,1024]{2,1,0:T(8,128)(2,1)S(1)} %bitcast.92), kind=kLoop, calls=%fused_computation.26 | loop fusion | flops 7864320 | bytes 10496000 | tf_op jit(solution)/shard_map/convert_element_type | solution.py:18
  58.1 0.8 fusion.27
  58.9 0.1 convert_reduce_fusion
  59.0 0.6 reduce_max.18
  59.7 0.6 reduce_max.19
  60.3 10.4 %convolution_bitcast_fusion.3.anchor_ref = bf16[8,512,1024]{2,1,0:T(8,128)(2,1)} fusion(bf16[320,8,1024]{2,0,1:T(8,128)(2,1)} %fusion.15, s32[512]{0:T(512)S(1)} %copy-done.6, pred[512]{0:T(512)(128)(4,1)S(1)} %iota_compare_fusion.17), kind=kOutput, calls=%fused_computation.28 | convolution fusion | flops 2684682240 | bytes 13634048 | tf_op jit(solution)/shard_map/sc,cwf->wsf/dot_general | solution.py:215
  71.9 10.2 %convolution_bitcast_fusion.2.own_ref = bf16[8,512,1024]{2,1,0:T(8,128)(2,1)} fusion(bf16[320,8,1024]{2,0,1:T(8,128)(2,1)} %fusion.15, s32[512]{0:T(512)S(1)} %copy-done.4, pred[512]{0:T(512)(128)(4,1)S(1)} %get-tuple-element.74), kind=kOutput, calls=%fused_computation.27 | convolution fusion | flops 2684682240 | bytes 13634048 | tf_op jit(solution)/shard_map/sc,cwf->wsf/dot_general | solution.py:215
  82.1 11.7 %collective-permute-done.5.af_ref = bf16[4,160,1024]{2,1,0:T(8,128)(2,1)} collective-permute-done((bf16[4,160,1024]{2,1,0:T(8,128)(2,1)S(1)}, bf16[4,160,1024]{2,1,0:T(8,128)(2,1)}, u32[]{:S(2)}, u32[]{:S(2)}) %collective-permute-start.5) | collective-permute-done | bytes 1310752 | tf_op jit(solution)/shard_map/ppermute | solution.py:81
  93.8 4.2 %collective-permute-done.4.bf_ref = bf16[4,160,1024]{2,1,0:T(8,128)(2,1)} collective-permute-done((bf16[4,160,1024]{2,1,0:T(8,128)(2,1)S(1)}, bf16[4,160,1024]{2,1,0:T(8,128)(2,1)}, u32[]{:S(2)}, u32[]{:S(2)}) %collective-permute-start.4) | collective-permute-done | bytes 1310752 | tf_op jit(solution)/shard_map/ppermute | solution.py:81
  98.0 0.4 conditional.1
  98.0 0.1 broadcast.209
  98.3 9.1 %shard_map.86 = f32[4,512,128]{2,1,0:T(8,128)} custom-call(bf16[8,512,1024]{2,1,0:T(8,128)(2,1)} %convolution_bitcast_fusion.3.anchor_ref, bf16[8,512,1024]{2,1,0:T(8,128)(2,1)} %convolution_bitcast_fusion.2.own_ref, bf16[512,160]{1,0:T(8,128)(2,1)} %get-tuple-element.91.sbf_ref, bf16[512,160]{1,0:T(8,128)(2,1)} %get-tuple-element.92.saf_ref, ...), custom_call_target="tpu_custom_call" | custom-call | tf_op jit(solution)/shard_map/pallas_call | solution.py:153
  107.5 16.6 %collective-permute-done.7.af_ref = bf16[4,160,1024]{2,1,0:T(8,128)(2,1)} collective-permute-done((bf16[4,160,1024]{2,1,0:T(8,128)(2,1)}, bf16[4,160,1024]{2,1,0:T(8,128)(2,1)}, u32[]{:S(2)}, u32[]{:S(2)}) %collective-permute-start.7) | collective-permute-done | bytes 1310752 | tf_op jit(solution)/shard_map/ppermute | solution.py:81
  124.0 27.5 %collective-permute-done.6.bf_ref = bf16[4,160,1024]{2,1,0:T(8,128)(2,1)} collective-permute-done((bf16[4,160,1024]{2,1,0:T(8,128)(2,1)}, bf16[4,160,1024]{2,1,0:T(8,128)(2,1)}, u32[]{:S(2)}, u32[]{:S(2)}) %collective-permute-start.6) | collective-permute-done | bytes 1310752 | tf_op jit(solution)/shard_map/ppermute | solution.py:81
  151.5 9.1 %shard_map.87 = f32[4,512,128]{2,1,0:T(8,128)} custom-call(bf16[8,512,1024]{2,1,0:T(8,128)(2,1)} %convolution_bitcast_fusion.3.anchor_ref, bf16[8,512,1024]{2,1,0:T(8,128)(2,1)} %convolution_bitcast_fusion.2.own_ref, bf16[512,160]{1,0:T(8,128)(2,1)} %get-tuple-element.91.sbf_ref, bf16[512,160]{1,0:T(8,128)(2,1)} %get-tuple-element.92.saf_ref, ...), custom_call_target="tpu_custom_call" | custom-call | tf_op jit(solution)/shard_map/pallas_call | solution.py:153
  160.7 1.5 fusion.85
  162.3 1.5 collective-permute-done.8
  163.8 1.6 collective-permute-start.9
  165.4 0.2 select_reduce_fusion.2
  165.5 6.7 %collective-permute-done.9 = f32[512,128]{1,0:T(8,128)S(1)} collective-permute-done((f32[512,128]{1,0:T(8,128)S(1)}, f32[512,128]{1,0:T(8,128)S(1)}, u32[]{:S(2)}, u32[]{:S(2)}) %collective-permute-start.9) | collective-permute-done | bytes 262176 | tf_op jit(solution)/shard_map/ppermute | solution.py:72
  172.2 0.1 multiply_reduce_fusion.3
  172.4 1.2 multiply_reduce_fusion.2
  173.7 0.7 multiply_reduce_fusion
  174.5 1.5 collective-permute-done.10
  176.0 1.6 collective-permute-start.11
  177.6 1.2 collective-permute-done.12
  178.7 0.5 collective-permute-start.13
  179.3 5.2 %collective-permute-done.13 = f32[512]{0:T(512)S(1)} collective-permute-done((f32[512]{0:T(512)S(1)}, f32[512]{0:T(512)S(1)}, u32[]{:S(2)}, u32[]{:S(2)}) %collective-permute-start.13) | collective-permute-done | bytes 2080 | tf_op jit(solution)/shard_map/ppermute | solution.py:72
  184.5 1.0 divide_select_fusion
  (67 shorter events, 1.4 us)
Async XLA Ops:
  2.0 15.5 %collective-permute-start.2 = (s32[1,1025]{1,0:T(1,128)S(1)}, s32[1,1025]{1,0:T(1,128)S(1)}, u32[]{:S(2)}, u32[]{:S(2)}) collective-permute-start(s32[1,1025]{1,0:T(1,128)S(1)} %broadcast_in_dim.41), channel_id=1, source_target_pairs={{0,4},{4,0},{8,12},{12,8},{1,5},{5,1},{9,13},{13,9},{2,6},{6,2},{1... | collective-permute-start | bytes 12308 | tf_op jit(solution)/shard_map/ppermute | solution.py:93
  5.1 8.2 %copy-start.5 = (s32[512]{0:T(512)S(1)}, s32[512]{0:T(512)}, u32[]{:S(2)}) copy-start(s32[512]{0:T(512)} %param.11) | copy-start | bytes 6148
  5.1 8.2 %copy-start.4 = (s32[512]{0:T(512)S(1)}, s32[512]{0:T(512)}, u32[]{:S(2)}) copy-start(s32[512]{0:T(512)} %param.12) | copy-start | bytes 6148
  17.5 4.6 %collective-permute-start.3 = (s32[2,1025]{1,0:T(2,128)S(1)}, s32[2,1025]{1,0:T(2,128)S(1)}, u32[]{:S(2)}, u32[]{:S(2)}) collective-permute-start(s32[2,1025]{1,0:T(2,128)S(1)} %add_select_fusion.1), channel_id=1, source_target_pairs={{0,8},{4,12},{8,0},{12,4},{1,9},{5,13},{9,1},{13,5},{2,10},{6,14},... | collective-permute-start | bytes 24608 | tf_op jit(solution)/shard_map/ppermute | solution.py:93
  25.9 3.8 %copy-start.3 = (bf16[320,4,1024]{2,1,0:T(4,128)(2,1)S(1)}, bf16[320,4,1024]{2,1,0:T(4,128)(2,1)}, u32[]{:S(2)}) copy-start(bf16[320,4,1024]{2,1,0:T(4,128)(2,1)} %get-tuple-element.64) | copy-start | bytes 7864324
  33.6 12.3 %slice-start = ((s8[5242880]{0:T(1024)(128)(4,1)}), s8[4194304]{0:T(1024)(128)(4,1)S(1)}, s32[]{:S(2)}) async-start(s8[5242880]{0:T(1024)(128)(4,1)} %bitcast.91), calls=%async_computation | async-start | bytes 8388608
  35.6 10.3 %slice-start.1 = ((s8[5242880]{0:T(1024)(128)(4,1)}), s8[1048576]{0:T(1024)(128)(4,1)S(1)}, s32[]{:S(2)}) async-start(s8[5242880]{0:T(1024)(128)(4,1)} %bitcast.91), calls=%async_computation.1 | async-start | bytes 2097152
  35.9 57.9 %collective-permute-start.5 = (bf16[4,160,1024]{2,1,0:T(8,128)(2,1)S(1)}, bf16[4,160,1024]{2,1,0:T(8,128)(2,1)}, u32[]{:S(2)}, u32[]{:S(2)}) collective-permute-start(bf16[4,160,1024]{2,1,0:T(8,128)(2,1)S(1)} %fusion.21), channel_id=1, source_target_pairs={{4,0},{8,4},{12,8},{0,12},{5,1},{9,5},{13,9},{1,13},{6,2},{10,6},{... | collective-permute-start | bytes 3932168 | tf_op jit(solution)/shard_map/ppermute | solution.py:81
  38.7 59.2 %collective-permute-start.4 = (bf16[4,160,1024]{2,1,0:T(8,128)(2,1)S(1)}, bf16[4,160,1024]{2,1,0:T(8,128)(2,1)}, u32[]{:S(2)}, u32[]{:S(2)}) collective-permute-start(bf16[4,160,1024]{2,1,0:T(8,128)(2,1)S(1)} %fusion.23), channel_id=1, source_target_pairs={{0,4},{4,8},{8,12},{12,0},{1,5},{5,9},{9,13},{13,1},{2,6},{6,10},{... | collective-permute-start | bytes 3932168 | tf_op jit(solution)/shard_map/ppermute | solution.py:81
  40.2 83.8 %collective-permute-start.7 = (bf16[4,160,1024]{2,1,0:T(8,128)(2,1)}, bf16[4,160,1024]{2,1,0:T(8,128)(2,1)}, u32[]{:S(2)}, u32[]{:S(2)}) collective-permute-start(bf16[4,160,1024]{2,1,0:T(8,128)(2,1)} %fusion.17), channel_id=1, source_target_pairs={{4,0},{8,4},{12,8},{0,12},{5,1},{9,5},{13,9},{1,13},{6,2},{10,6},{... | collective-permute-start | bytes 3932168 | tf_op jit(solution)/shard_map/ppermute | solution.py:81
  45.4 106.1 %collective-permute-start.6 = (bf16[4,160,1024]{2,1,0:T(8,128)(2,1)}, bf16[4,160,1024]{2,1,0:T(8,128)(2,1)}, u32[]{:S(2)}, u32[]{:S(2)}) collective-permute-start(bf16[4,160,1024]{2,1,0:T(8,128)(2,1)} %fusion.19), channel_id=1, source_target_pairs={{0,4},{4,8},{8,12},{12,0},{1,5},{5,9},{9,13},{13,1},{2,6},{6,10},{... | collective-permute-start | bytes 3932168 | tf_op jit(solution)/shard_map/ppermute | solution.py:81
  51.4 8.9 %copy-start.6 = (s32[512]{0:T(512)S(1)}, s32[512]{0:T(512)}, u32[]{:S(2)}) copy-start(s32[512]{0:T(512)} %param.10) | copy-start | bytes 6148
  107.4 53.2 %copy-start.1 = (f32[4,512,128]{2,1,0:T(8,128)S(1)}, f32[4,512,128]{2,1,0:T(8,128)}, u32[]{:S(2)}) copy-start(f32[4,512,128]{2,1,0:T(8,128)} %shard_map.86) | copy-start | bytes 3145732
  160.6 4.7 %copy-start.7 = (f32[8]{0:T(128)S(1)}, f32[8]{0:T(128)}, u32[]{:S(2)}) copy-start(f32[8]{0:T(128)} %param.15) | copy-start | bytes 100
  160.6 4.7 %copy-start.8 = (s32[8]{0:T(128)S(1)}, s32[8]{0:T(128)}, u32[]{:S(2)}) copy-start(s32[8]{0:T(128)} %param.14) | copy-start | bytes 100
  162.2 1.6 collective-permute-start.8
  163.8 8.4 %collective-permute-start.9 = (f32[512,128]{1,0:T(8,128)S(1)}, f32[512,128]{1,0:T(8,128)S(1)}, u32[]{:S(2)}, u32[]{:S(2)}) collective-permute-start(f32[512,128]{1,0:T(8,128)S(1)} %add.126), channel_id=1, source_target_pairs={{0,2},{1,3},{2,0},{3,1},{4,6},{5,7},{6,4},{7,5},{8,10},{9,11},{10,... | collective-permute-start | bytes 786440 | tf_op jit(solution)/shard_map/ppermute | solution.py:72
  174.4 1.6 collective-permute-start.10
  176.0 8.5 %collective-permute-start.11 = (f32[512,128]{1,0:T(8,128)S(1)}, f32[512,128]{1,0:T(8,128)S(1)}, u32[]{:S(2)}, u32[]{:S(2)}) collective-permute-start(f32[512,128]{1,0:T(8,128)S(1)} %add.132), channel_id=1, source_target_pairs={{0,2},{1,3},{2,0},{3,1},{4,6},{5,7},{6,4},{7,5},{8,10},{9,11},{10,... | collective-permute-start | bytes 786440 | tf_op jit(solution)/shard_map/ppermute | solution.py:72
  177.6 1.2 collective-permute-start.12
  178.7 5.7 %collective-permute-start.13 = (f32[512]{0:T(512)S(1)}, f32[512]{0:T(512)S(1)}, u32[]{:S(2)}, u32[]{:S(2)}) collective-permute-start(f32[512]{0:T(512)S(1)} %add.134), channel_id=1, source_target_pairs={{0,2},{1,3},{2,0},{3,1},{4,6},{5,7},{6,4},{7,5},{8,10},{9,11},{10,... | collective-permute-start | bytes 6152 | tf_op jit(solution)/shard_map/ppermute | solution.py:72
where the time goes:
time: 189 us; the launch traced here: 186 us
  waiting for transfers between devices  77.9 us (41%)
  matrix products  30.3 us (16%)
  other arithmetic  29.7 us (16%)
  Pallas kernels  18.3 us (10%)
  starting transfers between devices  16.3 us (9%)
  local copies, waits for them, and re-layouts  9.98 us (5%)
  between operations  3.05 us (2%)
    ppermute x2, waiting for transfers between devices, ring_exchange(): lax.ppermute(up_rows, axis, up)  31.7 us
    ppermute x2, waiting for transfers between devices, ring_exchange(): lax.ppermute(down_rows, axis, down)  28.3 us
    dot_general x2, matrix products, pick(): jnp.einsum('sc,cwf->wsf', selector.astype(jnp.bfloat16), rows, preferred_...  20.6 us
    pallas_call x2, Pallas kernels, halo_cross(): pl.pallas_call(cross_kernel, grid=(slots // group,), in_specs=[row_spec,...  18.3 us
    ppermute x6, waiting for transfers between devices, butterfly_sum(): value = jax.tree.map(jnp.add, value, lax.ppermute(value, axis, pairs))  16.1 us
    convert_element_type x5, other arithmetic, whiten(): return (spectra_f * lax.rsqrt(power_mean + EPS_POWER)).astype(jnp.bfloat16)  9.88 us
    slice x1, local copies, waits for them, and re-layouts, local(): spectra[:, c * chunk_wins:(c + 1) * chunk_wins]  8.17 us
    ppermute x2, starting transfers between devices, ring_exchange(): lax.ppermute(down_rows, axis, down)  6.33 us
  transfers between devices with their start and end apart: 12, of which 10 were waited for; matrix products, arithmetic and copies ran while one was open for 27% of the time, Pallas kernels for 5%

commit v1 on v0

--- a/solution.py
+++ b/solution.py
@@ -121,7 +121,7 @@
     return need_minus, need_plus, pos_minus, pos_plus
 
 
-def cross_kernel(anchor_ref, own_ref, sbf_ref, saf_ref, bf_ref, af_ref, t_ref, corr_ref):
+def cross_kernel(anchor_ref, own_ref, sbf_ref, saf_ref, bf_ref, af_ref, t_ref, corr_ref, sum_ref):
     wins = anchor_ref.shape[0]
     half = anchor_ref.shape[2] // 2
     t_re = t_ref[:half, :]
@@ -138,9 +138,12 @@
         p_re, p_im = part[:, :half], part[:, half:]
         c_re = (a_re * p_re + a_im * p_im).astype(jnp.bfloat16)
         c_im = (a_im * p_re - a_re * p_im).astype(jnp.bfloat16)
-        corr_ref[w] = jnp.dot(c_re, t_re, preferred_element_type=jnp.float32) + jnp.dot(
+        value = jnp.dot(c_re, t_re, preferred_element_type=jnp.float32) + jnp.dot(
             c_im, t_im, preferred_element_type=jnp.float32
         )
+        corr_ref[w] = value
+        total = value if w == 0 else total + value
+    sum_ref[...] = total
 
 
 def halo_cross(chunk, wins, anchors, own, sels, bufs, transform):
@@ -154,8 +157,14 @@
         cross_kernel,
         grid=(slots // group,),
         in_specs=[row_spec, row_spec] + sel_specs + buf_specs + [pl.BlockSpec(transform.shape, lambda i: (0, 0))],
-        out_specs=pl.BlockSpec((wins, group, lag_count), lambda i: (0, i, 0)),
-        out_shape=jax.ShapeDtypeStruct((wins, slots, lag_count), jnp.float32),
+        out_specs=[
+            pl.BlockSpec((wins, group, lag_count), lambda i: (0, i, 0)),
+            pl.BlockSpec((group, lag_count), lambda i: (i, 0)),
+        ],
+        out_shape=[
+            jax.ShapeDtypeStruct((wins, slots, lag_count), jnp.float32),
+            jax.ShapeDtypeStruct((slots, lag_count), jnp.float32),
+        ],
         compiler_params=pltpu.CompilerParams(vmem_limit_bytes=56 * 1024 * 1024),
     )(anchors, own, *sels, *bufs, transform)
 
@@ -225,10 +234,11 @@
         onehot(before_row, fast_rows, use_before).astype(jnp.bfloat16),
         onehot(after_row, fast_rows, use_after).astype(jnp.bfloat16),
     ]
-    corr_full = jnp.concatenate([
+    fast_out = [
         halo_cross(c, chunk_wins, anchors, own, sels, [fast[c][0], fast[c][1]], transform)
         for c in range(chunks)
-    ])
+    ]
+    corr_full = jnp.concatenate([corr for corr, _ in fast_out])
 
     def spill_extra(_):
         (got_before, got_after), _ = gather_rows(fast_rows, spill_rows, white, whitened=True)
@@ -237,21 +247,23 @@
             onehot(after_row - fast_rows, spill_rows, use_after).astype(jnp.bfloat16),
         ]
         zero_own = jnp.zeros_like(own)
-        extra = jnp.concatenate([
+        outs = [
             halo_cross(c, chunk_wins, anchors, zero_own, spill_sels,
                        [got_before[c * chunk_wins:(c + 1) * chunk_wins], got_after[c * chunk_wins:(c + 1) * chunk_wins]],
                        transform)
             for c in range(chunks)
-        ])
-        return extra
+        ]
+        return jnp.concatenate([corr for corr, _ in outs]), sum(part for _, part in outs)
 
     def no_extra(_):
-        return jnp.zeros((local_wins, pair_slots, lag_count), jnp.float32)
+        return (jnp.zeros((local_wins, pair_slots, lag_count), jnp.float32),
+                jnp.zeros((pair_slots, lag_count), jnp.float32))
 
     spill_late, _ = lax.optimization_barrier((spill, fast[0]))
-    corr_full = corr_full + lax.cond(spill_late, spill_extra, no_extra, 0)
+    extra, extra_sum = lax.cond(spill_late, spill_extra, no_extra, 0)
+    corr_full = corr_full + extra
     corr_all = lax.reduce_precision(corr_full, exponent_bits=8, mantissa_bits=7)
-    running = jnp.sum(corr_full, axis=0)
+    running = sum(part for _, part in fast_out) + extra_sum
 
     ref_sum = butterfly_sum(running, "win")
     norm_scale = jnp.sqrt(jnp.float32(local_wins * lax.axis_size("win")))

time: 189 us -> 199 us (1.053)
  waiting for transfers between devices: 77.9 us -> 86.4 us
    ppermute x2, waiting for transfers between devices: 28.3 us -> 41 us  [ring_exchange(): lax.ppermute(down_rows, axis, down)]
    ppermute x2, waiting for transfers between devices: 31.7 us -> 27.4 us  [ring_exchange(): lax.ppermute(up_rows, axis, up)]
    convert_element_type x5, other arithmetic: 9.88 us -> 12 us  [whiten(): return (spectra_f * lax.rsqrt(power_mean + EPS_POWER)).astype(jnp.bfloat16)]
  transfers between devices with their start and end apart: 12 -> 12, of which waited for: 10 -> 8; matrix products, arithmetic and copies ran while one was open for 27% -> 27% of each run, Pallas kernels for 5% -> 5%
where the time goes in v1:
time: 199 us; the launch traced here: 196 us
  waiting for transfers between devices  86.4 us (43%)
  other arithmetic  31.6 us (16%)
  matrix products  28.4 us (14%)
  Pallas kernels  18.4 us (9%)
  starting transfers between devices  16.2 us (8%)
  local copies, waits for them, and re-layouts  11.1 us (6%)
  between operations  3.12 us (2%)
    ppermute x2, waiting for transfers between devices, ring_exchange(): lax.ppermute(down_rows, axis, down)  41 us
    ppermute x2, waiting for transfers between devices, ring_exchange(): lax.ppermute(up_rows, axis, up)  27.4 us
    dot_general x2, matrix products, pick(): jnp.einsum('sc,cwf->wsf', selector.astype(jnp.bfloat16), rows, preferred_...  20.6 us
    pallas_call x2, Pallas kernels, halo_cross(): pl.pallas_call(cross_kernel, grid=(slots // group,), in_specs=[row_spec,...  18.4 us
    ppermute x6, waiting for transfers between devices, butterfly_sum(): value = jax.tree.map(jnp.add, value, lax.ppermute(value, axis, pairs))  16.1 us
    convert_element_type x5, other arithmetic, whiten(): return (spectra_f * lax.rsqrt(power_mean + EPS_POWER)).astype(jnp.bfloat16)  12 us
    slice x1, local copies, waits for them, and re-layouts, local(): spectra[:, c * chunk_wins:(c + 1) * chunk_wins]  8.17 us
    ppermute x2, starting transfers between devices, ring_exchange(): lax.ppermute(down_rows, axis, down)  6.3 us
  transfers between devices with their start and end apart: 12, of which 8 were waited for; matrix products, arithmetic and copies ran while one was open for 27% of the time, Pallas kernels for 5%

profile of v1, /device:TPU:0, one launch (start us, length us, event | category | flops | bytes accessed | tf_op | source)
XLA Modules:
  0.0 195.5 jit_solution(8531317813748960735)
XLA Ops:
  1.3 0.7 pad_add_fusion
  2.0 3.1 %collective-permute-start.2 = (s32[1,1025]{1,0:T(1,128)S(1)}, s32[1,1025]{1,0:T(1,128)S(1)}, u32[]{:S(2)}, u32[]{:S(2)}) collective-permute-start(s32[1,1025]{1,0:T(1,128)S(1)} %broadcast_in_dim.41), channel_id=1, source_target_pairs={{0,4},{4,0},{8,12},{12,8},{1,5},{5,1},{9,13},{13,9},{2,6},{6,2},{1... | collective-permute-start | bytes 12308 | tf_op jit(solution)/shard_map/ppermute | solution.py:93
  5.1 8.2 %fusion.88 = (bf16[320,4,1024]{2,1,0:T(4,128)(2,1)S(1)}, bf16[320,4,1024]{2,1,0:T(4,128)(2,1)}) fusion(bf16[320,8,1024]{2,1,0:T(8,128)(2,1)} %param.9), kind=kLoop, calls=%fused_computation.167 | loop fusion | bytes 10485760 | tf_op jit(solution)/shard_map/slice | solution.py:211
  13.3 0.2 fusion.51
  13.6 0.3 reduce-window.50
  14.0 0.1 slice_reduce_fusion.1
  14.2 0.3 reduce-window.48
  14.6 0.1 slice_reduce_fusion.2
  14.8 0.2 select_reduce_fusion
  15.0 1.1 fusion.53
  16.2 1.3 fusion.61
  17.5 2.7 %collective-permute-start.3 = (s32[2,1025]{1,0:T(2,128)S(1)}, s32[2,1025]{1,0:T(2,128)S(1)}, u32[]{:S(2)}, u32[]{:S(2)}) collective-permute-start(s32[2,1025]{1,0:T(2,128)S(1)} %add_select_fusion.1), channel_id=1, source_target_pairs={{0,8},{4,12},{8,0},{12,4},{1,9},{5,13},{9,1},{13,5},{2,10},{6,14},... | collective-permute-start | bytes 24608 | tf_op jit(solution)/shard_map/ppermute | solution.py:93
  20.2 1.9 collective-permute-done.3
  22.2 0.7 fusion.89
  22.9 0.1 fusion.90
  23.0 1.3 fusion.83
  24.2 0.2 fusion.44
  24.4 0.3 reduce-window.36
  24.8 0.1 slice_reduce_fusion.3
  25.0 0.2 fusion.42
  25.2 0.3 reduce-window.34
  25.7 0.1 slice_reduce_fusion.4
  25.9 2.0 %fusion.16 = (f32[4,160]{1,0:T(4,128)S(1)}, bf16[160,4,1024]{2,0,1:T(8,128)(2,1)S(1)}) fusion(bf16[320,4,1024]{2,1,0:T(4,128)(2,1)S(1)} %get-tuple-element.75, s32[320]{0:T(512)S(1)} %slice_add_fusion.2, pred[320]{0:T(512)(128)(4,1)S(1)} %fusion.44), kind=kOutput, calls=%fused_computation.31 | convolution fusion | flops 421498240 | bytes 3936320 | tf_op jit(solution)/shard_map/jc,cwf->wjf/dot_general | solution.py:203
  27.8 2.0 fusion.18
  29.8 2.0 fusion.20
  31.8 1.9 fusion.22
  33.8 1.4 fusion.17
  35.2 2.5 %collective-permute-start.7 = (bf16[4,160,1024]{2,1,0:T(8,128)(2,1)}, bf16[4,160,1024]{2,1,0:T(8,128)(2,1)}, u32[]{:S(2)}, u32[]{:S(2)}) collective-permute-start(bf16[4,160,1024]{2,1,0:T(8,128)(2,1)} %fusion.17), channel_id=1, source_target_pairs={{4,0},{8,4},{12,8},{0,12},{5,1},{9,5},{13,9},{1,13},{6,2},{10,6},{... | collective-permute-start | bytes 3932168 | tf_op jit(solution)/shard_map/ppermute | solution.py:81
  37.6 1.4 fusion.19
  39.0 1.4 fusion.21
  40.4 3.8 %collective-permute-start.5 = (bf16[4,160,1024]{2,1,0:T(8,128)(2,1)}, bf16[4,160,1024]{2,1,0:T(8,128)(2,1)S(1)}, u32[]{:S(2)}, u32[]{:S(2)}) collective-permute-start(bf16[4,160,1024]{2,1,0:T(8,128)(2,1)} %fusion.21), channel_id=1, source_target_pairs={{4,0},{8,4},{12,8},{0,12},{5,1},{9,5},{13,9},{1,13},{6,2},{10,6},{... | collective-permute-start | bytes 3932168 | tf_op jit(solution)/shard_map/ppermute | solution.py:81
  44.2 1.3 fusion.23
  45.5 0.4 collective-permute-start.4
  45.9 0.1 slice_reduce_fusion
  46.1 5.5 %fusion.14 = f32[320,8]{0,1:T(8,128)S(1)} fusion(bf16[320,8,1024]{2,1,0:T(8,128)(2,1)S(1)} %bitcast.92), kind=kLoop, calls=%fused_computation.25 | loop fusion | flops 7861760 | bytes 5253120 | tf_op jit(solution)/shard_map/reduce_sum | solution.py:17
  51.6 6.5 %fusion.15 = bf16[320,8,1024]{2,0,1:T(8,128)(2,1)} fusion(f32[320,8]{0,1:T(8,128)S(1)} %add_rsqrt_fusion, bf16[320,8,1024]{2,1,0:T(8,128)(2,1)S(1)} %bitcast.92), kind=kLoop, calls=%fused_computation.26 | loop fusion | flops 7864320 | bytes 10496000 | tf_op jit(solution)/shard_map/convert_element_type | solution.py:18
  58.2 0.8 fusion.27
  59.0 0.1 convert_reduce_fusion
  59.2 0.7 reduce_max.18
  59.9 0.6 reduce_max.19
  60.5 10.4 %convolution_bitcast_fusion.3.anchor_ref = bf16[8,512,1024]{2,1,0:T(8,128)(2,1)} fusion(bf16[320,8,1024]{2,0,1:T(8,128)(2,1)} %fusion.15, s32[512]{0:T(512)S(1)} %copy-done.11, pred[512]{0:T(512)(128)(4,1)S(1)} %iota_compare_fusion.17), kind=kOutput, calls=%fused_computation.28 | convolution fusion | flops 2684682240 | bytes 13634048 | tf_op jit(solution)/shard_map/sc,cwf->wsf/dot_general | solution.py:224
  72.2 10.2 %convolution_bitcast_fusion.2.own_ref = bf16[8,512,1024]{2,1,0:T(8,128)(2,1)} fusion(bf16[320,8,1024]{2,0,1:T(8,128)(2,1)} %fusion.15, s32[512]{0:T(512)S(1)} %copy-done.9, pred[512]{0:T(512)(128)(4,1)S(1)} %get-tuple-element.85), kind=kOutput, calls=%fused_computation.27 | convolution fusion | flops 2684682240 | bytes 13634048 | tf_op jit(solution)/shard_map/sc,cwf->wsf/dot_general | solution.py:224
  82.4 41.0 %collective-permute-done.5.af_ref = bf16[4,160,1024]{2,1,0:T(8,128)(2,1)S(1)} collective-permute-done((bf16[4,160,1024]{2,1,0:T(8,128)(2,1)}, bf16[4,160,1024]{2,1,0:T(8,128)(2,1)S(1)}, u32[]{:S(2)}, u32[]{:S(2)}) %collective-permute-start.5) | collective-permute-done | bytes 1310752 | tf_op jit(solution)/shard_map/ppermute | solution.py:81
  123.4 27.4 %collective-permute-done.4.bf_ref = bf16[4,160,1024]{2,1,0:T(8,128)(2,1)S(1)} collective-permute-done((bf16[4,160,1024]{2,1,0:T(8,128)(2,1)}, bf16[4,160,1024]{2,1,0:T(8,128)(2,1)S(1)}, u32[]{:S(2)}, u32[]{:S(2)}) %collective-permute-start.4) | collective-permute-done | bytes 1310752 | tf_op jit(solution)/shard_map/ppermute | solution.py:81
  150.8 1.1 copy-done.5
  151.9 0.4 conditional.1
  151.9 0.1 broadcast.211
  152.3 9.2 %shard_map.86 = (f32[4,512,128]{2,1,0:T(8,128)}, f32[512,128]{1,0:T(8,128)}) custom-call(bf16[8,512,1024]{2,1,0:T(8,128)(2,1)} %convolution_bitcast_fusion.3.anchor_ref, bf16[8,512,1024]{2,1,0:T(8,128)(2,1)} %convolution_bitcast_fusion.2.own_ref, bf16[512,160]{1,0:T(8,128)(2,1)} %get-tuple-element.102.sbf_ref, bf16[512,160]{1,0:T(8,128)(2,1)} %get-tuple-element.103.saf_ref, ...), custom_call_target="tpu_custom_call" | custom-call | tf_op jit(solution)/shard_map/pallas_call | solution.py:156
  161.5 9.3 %shard_map.87 = (f32[4,512,128]{2,1,0:T(8,128)}, f32[512,128]{1,0:T(8,128)}) custom-call(bf16[8,512,1024]{2,1,0:T(8,128)(2,1)} %convolution_bitcast_fusion.3.anchor_ref, bf16[8,512,1024]{2,1,0:T(8,128)(2,1)} %convolution_bitcast_fusion.2.own_ref, bf16[512,160]{1,0:T(8,128)(2,1)} %get-tuple-element.102.sbf_ref, bf16[512,160]{1,0:T(8,128)(2,1)} %get-tuple-element.103.saf_ref, ...), custom_call_target="tpu_custom_call" | custom-call | tf_op jit(solution)/shard_map/pallas_call | solution.py:156
  170.8 1.1 add_add_fusion
  172.0 1.5 collective-permute-done.8
  173.6 1.6 collective-permute-start.9
  175.1 0.2 select_reduce_fusion.2
  175.3 6.7 %collective-permute-done.9 = f32[512,128]{1,0:T(8,128)S(1)} collective-permute-done((f32[512,128]{1,0:T(8,128)S(1)}, f32[512,128]{1,0:T(8,128)S(1)}, u32[]{:S(2)}, u32[]{:S(2)}) %collective-permute-start.9) | collective-permute-done | bytes 262176 | tf_op jit(solution)/shard_map/ppermute | solution.py:72
  182.0 0.1 multiply_reduce_fusion.3
  182.2 1.2 multiply_reduce_fusion.2
  183.4 0.1 fusion.85
  183.4 0.7 multiply_reduce_fusion
  184.3 1.5 collective-permute-done.10
  185.8 1.6 collective-permute-start.11
  187.4 1.2 collective-permute-done.12
  188.5 0.5 collective-permute-start.13
  189.1 5.2 %collective-permute-done.13 = f32[512]{0:T(512)S(1)} collective-permute-done((f32[512]{0:T(512)S(1)}, f32[512]{0:T(512)S(1)}, u32[]{:S(2)}, u32[]{:S(2)}) %collective-permute-start.13) | collective-permute-done | bytes 2080 | tf_op jit(solution)/shard_map/ppermute | solution.py:72
  194.3 1.0 divide_select_fusion
  (76 shorter events, 1.4 us)
Async XLA Ops:
  2.0 15.5 %collective-permute-start.2 = (s32[1,1025]{1,0:T(1,128)S(1)}, s32[1,1025]{1,0:T(1,128)S(1)}, u32[]{:S(2)}, u32[]{:S(2)}) collective-permute-start(s32[1,1025]{1,0:T(1,128)S(1)} %broadcast_in_dim.41), channel_id=1, source_target_pairs={{0,4},{4,0},{8,12},{12,8},{1,5},{5,1},{9,13},{13,9},{2,6},{6,2},{1... | collective-permute-start | bytes 12308 | tf_op jit(solution)/shard_map/ppermute | solution.py:93
  5.1 8.2 %copy-start.10 = (s32[512]{0:T(512)S(1)}, s32[512]{0:T(512)}, u32[]{:S(2)}) copy-start(s32[512]{0:T(512)} %param.11) | copy-start | bytes 6148
  5.1 8.2 %copy-start.9 = (s32[512]{0:T(512)S(1)}, s32[512]{0:T(512)}, u32[]{:S(2)}) copy-start(s32[512]{0:T(512)} %param.12) | copy-start | bytes 6148
  17.5 4.6 %collective-permute-start.3 = (s32[2,1025]{1,0:T(2,128)S(1)}, s32[2,1025]{1,0:T(2,128)S(1)}, u32[]{:S(2)}, u32[]{:S(2)}) collective-permute-start(s32[2,1025]{1,0:T(2,128)S(1)} %add_select_fusion.1), channel_id=1, source_target_pairs={{0,8},{4,12},{8,0},{12,4},{1,9},{5,13},{9,1},{13,5},{2,10},{6,14},... | collective-permute-start | bytes 24608 | tf_op jit(solution)/shard_map/ppermute | solution.py:93
  27.8 2.0 %copy-start.3 = (bf16[320,4,1024]{2,1,0:T(4,128)(2,1)S(1)}, bf16[320,4,1024]{2,1,0:T(4,128)(2,1)}, u32[]{:S(2)}) copy-start(bf16[320,4,1024]{2,1,0:T(4,128)(2,1)} %get-tuple-element.76) | copy-start | bytes 7864324
  31.7 14.3 %slice-start = ((s8[5242880]{0:T(1024)(128)(4,1)}), s8[4194304]{0:T(1024)(128)(4,1)S(1)}, s32[]{:S(2)}) async-start(s8[5242880]{0:T(1024)(128)(4,1)} %bitcast.91), calls=%async_computation | async-start | bytes 8388608
  33.8 12.3 %slice-start.1 = ((s8[5242880]{0:T(1024)(128)(4,1)}), s8[1048576]{0:T(1024)(128)(4,1)S(1)}, s32[]{:S(2)}) async-start(s8[5242880]{0:T(1024)(128)(4,1)} %bitcast.91), calls=%async_computation.1 | async-start | bytes 2097152
  35.2 126.3 %collective-permute-start.7 = (bf16[4,160,1024]{2,1,0:T(8,128)(2,1)}, bf16[4,160,1024]{2,1,0:T(8,128)(2,1)}, u32[]{:S(2)}, u32[]{:S(2)}) collective-permute-start(bf16[4,160,1024]{2,1,0:T(8,128)(2,1)} %fusion.17), channel_id=1, source_target_pairs={{4,0},{8,4},{12,8},{0,12},{5,1},{9,5},{13,9},{1,13},{6,2},{10,6},{... | collective-permute-start | bytes 3932168 | tf_op jit(solution)/shard_map/ppermute | solution.py:81
  39.0 122.5 %collective-permute-start.6 = (bf16[4,160,1024]{2,1,0:T(8,128)(2,1)}, bf16[4,160,1024]{2,1,0:T(8,128)(2,1)}, u32[]{:S(2)}, u32[]{:S(2)}) collective-permute-start(bf16[4,160,1024]{2,1,0:T(8,128)(2,1)} %fusion.19), channel_id=1, source_target_pairs={{0,4},{4,8},{8,12},{12,0},{1,5},{5,9},{9,13},{13,1},{2,6},{6,10},{... | collective-permute-start | bytes 3932168 | tf_op jit(solution)/shard_map/ppermute | solution.py:81
  40.4 83.0 %collective-permute-start.5 = (bf16[4,160,1024]{2,1,0:T(8,128)(2,1)}, bf16[4,160,1024]{2,1,0:T(8,128)(2,1)S(1)}, u32[]{:S(2)}, u32[]{:S(2)}) collective-permute-start(bf16[4,160,1024]{2,1,0:T(8,128)(2,1)} %fusion.21), channel_id=1, source_target_pairs={{4,0},{8,4},{12,8},{0,12},{5,1},{9,5},{13,9},{1,13},{6,2},{10,6},{... | collective-permute-start | bytes 3932168 | tf_op jit(solution)/shard_map/ppermute | solution.py:81
  45.5 105.3 %collective-permute-start.4 = (bf16[4,160,1024]{2,1,0:T(8,128)(2,1)}, bf16[4,160,1024]{2,1,0:T(8,128)(2,1)S(1)}, u32[]{:S(2)}, u32[]{:S(2)}) collective-permute-start(bf16[4,160,1024]{2,1,0:T(8,128)(2,1)} %fusion.23), channel_id=1, source_target_pairs={{0,4},{4,8},{8,12},{12,0},{1,5},{5,9},{9,13},{13,1},{2,6},{6,10},{... | collective-permute-start | bytes 3932168 | tf_op jit(solution)/shard_map/ppermute | solution.py:81
  51.6 9.0 %copy-start.11 = (s32[512]{0:T(512)S(1)}, s32[512]{0:T(512)}, u32[]{:S(2)}) copy-start(s32[512]{0:T(512)} %param.10) | copy-start | bytes 6148
  123.4 27.4 %copy-start.4 = (bf16[4,160,1024]{2,1,0:T(8,128)(2,1)}, bf16[4,160,1024]{2,1,0:T(8,128)(2,1)S(1)}, u32[]{:S(2)}) copy-start(bf16[4,160,1024]{2,1,0:T(8,128)(2,1)S(1)} %collective-permute-done.5.af_ref) | copy-start | bytes 3932164
  150.8 1.1 copy-start.5
  161.5 9.3 %copy-start.8 = (f32[512,128]{1,0:T(8,128)S(1)}, f32[512,128]{1,0:T(8,128)}, u32[]{:S(2)}) copy-start(f32[512,128]{1,0:T(8,128)} %get-tuple-element.48) | copy-start | bytes 786436
  161.5 13.7 %copy-start.12 = (f32[8]{0:T(128)S(1)}, f32[8]{0:T(128)}, u32[]{:S(2)}) copy-start(f32[8]{0:T(128)} %param.15) | copy-start | bytes 100
  161.5 13.7 %copy-start.13 = (s32[8]{0:T(128)S(1)}, s32[8]{0:T(128)}, u32[]{:S(2)}) copy-start(s32[8]{0:T(128)} %param.14) | copy-start | bytes 100
  170.8 11.4 %copy-start.1 = (f32[4,512,128]{2,1,0:T(8,128)S(1)}, f32[4,512,128]{2,1,0:T(8,128)}, u32[]{:S(2)}) copy-start(f32[4,512,128]{2,1,0:T(8,128)} %get-tuple-element.52) | copy-start | bytes 3145732
  170.8 11.4 %copy-start.2 = (f32[4,512,128]{2,1,0:T(8,128)S(1)}, f32[4,512,128]{2,1,0:T(8,128)}, u32[]{:S(2)}) copy-start(f32[4,512,128]{2,1,0:T(8,128)} %get-tuple-element.53) | copy-start | bytes 3145732
  171.9 1.6 collective-permute-start.8
  173.6 8.4 %collective-permute-start.9 = (f32[512,128]{1,0:T(8,128)S(1)}, f32[512,128]{1,0:T(8,128)S(1)}, u32[]{:S(2)}, u32[]{:S(2)}) collective-permute-start(f32[512,128]{1,0:T(8,128)S(1)} %add.136), channel_id=1, source_target_pairs={{0,2},{1,3},{2,0},{3,1},{4,6},{5,7},{6,4},{7,5},{8,10},{9,11},{10,... | collective-permute-start | bytes 786440 | tf_op jit(solution)/shard_map/ppermute | solution.py:72
  184.2 1.6 collective-permute-start.10
  185.8 8.5 %collective-permute-start.11 = (f32[512,128]{1,0:T(8,128)S(1)}, f32[512,128]{1,0:T(8,128)S(1)}, u32[]{:S(2)}, u32[]{:S(2)}) collective-permute-start(f32[512,128]{1,0:T(8,128)S(1)} %add.143), channel_id=1, source_target_pairs={{0,2},{1,3},{2,0},{3,1},{4,6},{5,7},{6,4},{7,5},{8,10},{9,11},{10,... | collective-permute-start | bytes 786440 | tf_op jit(solution)/shard_map/ppermute | solution.py:72
  187.4 1.2 collective-permute-start.12
  188.5 5.7 %collective-permute-start.13 = (f32[512]{0:T(512)S(1)}, f32[512]{0:T(512)S(1)}, u32[]{:S(2)}, u32[]{:S(2)}) collective-permute-start(f32[512]{0:T(512)S(1)} %add.145), channel_id=1, source_target_pairs={{0,2},{1,3},{2,0},{3,1},{4,6},{5,7},{6,4},{7,5},{8,10},{9,11},{10,... | collective-permute-start | bytes 6152 | tf_op jit(solution)/shard_map/ppermute | solution.py:72

commit v2 on v0

--- a/solution.py
+++ b/solution.py
@@ -146,7 +146,7 @@
 def halo_cross(chunk, wins, anchors, own, sels, bufs, transform):
     _, slots, width = anchors.shape
     lag_count = transform.shape[1]
-    group = min(256, slots)
+    group = min(512, slots)
     row_spec = pl.BlockSpec((wins, group, width), lambda i: (chunk, i, 0))
     sel_specs = [pl.BlockSpec((group, sel.shape[1]), lambda i: (i, 0)) for sel in sels]
     buf_specs = [pl.BlockSpec((wins,) + buf.shape[1:], lambda i: (0, 0, 0)) for buf in bufs]

time: 189 us -> 190 us (level)
  no operation moved by 1% of the time
where the time goes in v2:
time: 190 us; the launch traced here: 186 us
  waiting for transfers between devices  77.2 us (41%)
  matrix products  30.3 us (16%)
  other arithmetic  29.7 us (16%)
  Pallas kernels  19.7 us (10%)
  starting transfers between devices  16.3 us (9%)
  local copies, waits for them, and re-layouts  9.98 us (5%)
  between operations  3.04 us (2%)
    ppermute x2, waiting for transfers between devices, ring_exchange(): lax.ppermute(up_rows, axis, up)  31.7 us
    ppermute x2, waiting for transfers between devices, ring_exchange(): lax.ppermute(down_rows, axis, down)  27.5 us
    dot_general x2, matrix products, pick(): jnp.einsum('sc,cwf->wsf', selector.astype(jnp.bfloat16), rows, preferred_...  20.6 us
    pallas_call x2, Pallas kernels, halo_cross(): pl.pallas_call(cross_kernel, grid=(slots // group,), in_specs=[row_spec,...  19.7 us
    ppermute x6, waiting for transfers between devices, butterfly_sum(): value = jax.tree.map(jnp.add, value, lax.ppermute(value, axis, pairs))  16.1 us
    convert_element_type x5, other arithmetic, whiten(): return (spectra_f * lax.rsqrt(power_mean + EPS_POWER)).astype(jnp.bfloat16)  9.88 us
    slice x1, local copies, waits for them, and re-layouts, local(): spectra[:, c * chunk_wins:(c + 1) * chunk_wins]  8.17 us
    ppermute x2, starting transfers between devices, ring_exchange(): lax.ppermute(down_rows, axis, down)  6.33 us
  transfers between devices with their start and end apart: 12, of which 10 were waited for; matrix products, arithmetic and copies ran while one was open for 27% of the time, Pallas kernels for 5%

profile of v2, /device:TPU:0, one launch (start us, length us, event | category | flops | bytes accessed | tf_op | source)
XLA Modules:
  0.0 186.4 jit_solution(6508877587074605524)
XLA Ops:
  1.3 0.7 pad_add_fusion
  2.0 3.1 %collective-permute-start.2 = (s32[1,1025]{1,0:T(1,128)S(1)}, s32[1,1025]{1,0:T(1,128)S(1)}, u32[]{:S(2)}, u32[]{:S(2)}) collective-permute-start(s32[1,1025]{1,0:T(1,128)S(1)} %broadcast_in_dim.41), channel_id=1, source_target_pairs={{0,4},{4,0},{8,12},{12,8},{1,5},{5,1},{9,13},{13,9},{2,6},{6,2},{1... | collective-permute-start | bytes 12308 | tf_op jit(solution)/shard_map/ppermute | solution.py:93
  5.1 8.2 %fusion.88 = (bf16[320,4,1024]{2,1,0:T(4,128)(2,1)}, bf16[320,4,1024]{2,1,0:T(4,128)(2,1)S(1)}) fusion(bf16[320,8,1024]{2,1,0:T(8,128)(2,1)} %param.9), kind=kLoop, calls=%fused_computation.166 | loop fusion | bytes 10485760 | tf_op jit(solution)/shard_map/slice | solution.py:202
  13.3 0.2 fusion.50
  13.6 0.3 reduce-window.50
  14.0 0.1 slice_reduce_fusion.1
  14.2 0.3 reduce-window.48
  14.6 0.1 slice_reduce_fusion.2
  14.8 0.2 select_reduce_fusion
  15.0 1.1 fusion.52
  16.2 1.3 fusion.60
  17.5 2.7 %collective-permute-start.3 = (s32[2,1025]{1,0:T(2,128)S(1)}, s32[2,1025]{1,0:T(2,128)S(1)}, u32[]{:S(2)}, u32[]{:S(2)}) collective-permute-start(s32[2,1025]{1,0:T(2,128)S(1)} %add_select_fusion.1), channel_id=1, source_target_pairs={{0,8},{4,12},{8,0},{12,4},{1,9},{5,13},{9,1},{13,5},{2,10},{6,14},... | collective-permute-start | bytes 24608 | tf_op jit(solution)/shard_map/ppermute | solution.py:93
  20.2 1.9 %collective-permute-done.3 = s32[2,1025]{1,0:T(2,128)S(1)} collective-permute-done((s32[2,1025]{1,0:T(2,128)S(1)}, s32[2,1025]{1,0:T(2,128)S(1)}, u32[]{:S(2)}, u32[]{:S(2)}) %collective-permute-start.3) | collective-permute-done | bytes 8232 | tf_op jit(solution)/shard_map/ppermute | solution.py:93
  22.2 0.7 fusion.89
  22.9 0.1 fusion.90
  23.0 1.3 fusion.82
  24.2 0.2 fusion.43
  24.4 0.3 reduce-window.36
  24.8 0.1 slice_reduce_fusion.3
  25.0 0.2 fusion.41
  25.2 0.3 reduce-window.34
  25.7 0.1 slice_reduce_fusion.4
  25.9 3.8 %fusion.16 = (f32[4,160]{1,0:T(4,128)S(1)}, bf16[160,4,1024]{2,0,1:T(8,128)(2,1)S(1)}) fusion(bf16[320,4,1024]{2,1,0:T(4,128)(2,1)} %get-tuple-element.64, s32[320]{0:T(512)S(1)} %slice_add_fusion.2, pred[320]{0:T(512)(128)(4,1)S(1)} %fusion.43), kind=kOutput, calls=%fused_computation.31 | convolution fusion | flops 421498240 | bytes 3936320 | tf_op jit(solution)/shard_map/jc,cwf->wjf/dot_general | solution.py:194
  29.7 2.0 %fusion.18 = (f32[4,160]{1,0:T(4,128)S(1)}, bf16[160,4,1024]{2,0,1:T(8,128)(2,1)S(1)}) fusion(bf16[320,4,1024]{2,1,0:T(4,128)(2,1)S(1)} %copy-done.3, s32[320]{0:T(512)S(1)} %slice_add_fusion.3, pred[320]{0:T(512)(128)(4,1)S(1)} %fusion.41), kind=kOutput, calls=%fused_computation.35 | convolution fusion | flops 421498240 | bytes 3936320 | tf_op jit(solution)/shard_map/jc,cwf->wjf/dot_general | solution.py:192
  31.7 2.0 %fusion.20 = (f32[4,160]{1,0:T(4,128)S(1)}, bf16[160,4,1024]{2,0,1:T(8,128)(2,1)S(1)}) fusion(bf16[320,4,1024]{2,1,0:T(4,128)(2,1)S(1)} %get-tuple-element.65, s32[320]{0:T(512)S(1)} %slice_add_fusion.2, pred[320]{0:T(512)(128)(4,1)S(1)} %fusion.43), kind=kOutput, calls=%fused_computation.39 | convolution fusion | flops 421498240 | bytes 3936320 | tf_op jit(solution)/shard_map/jc,cwf->wjf/dot_general | solution.py:194
  33.6 2.0 %fusion.22 = (f32[4,160]{1,0:T(4,128)S(1)}, bf16[160,4,1024]{2,0,1:T(8,128)(2,1)S(1)}) fusion(bf16[320,4,1024]{2,1,0:T(4,128)(2,1)S(1)} %get-tuple-element.65, s32[320]{0:T(512)S(1)} %slice_add_fusion.3, pred[320]{0:T(512)(128)(4,1)S(1)} %fusion.41), kind=kOutput, calls=%fused_computation.43 | convolution fusion | flops 421498240 | bytes 3936320 | tf_op jit(solution)/shard_map/jc,cwf->wjf/dot_general | solution.py:192
  35.6 0.3 fusion.21
  35.9 2.5 %collective-permute-start.5 = (bf16[4,160,1024]{2,1,0:T(8,128)(2,1)S(1)}, bf16[4,160,1024]{2,1,0:T(8,128)(2,1)}, u32[]{:S(2)}, u32[]{:S(2)}) collective-permute-start(bf16[4,160,1024]{2,1,0:T(8,128)(2,1)S(1)} %fusion.21), channel_id=1, source_target_pairs={{4,0},{8,4},{12,8},{0,12},{5,1},{9,5},{13,9},{1,13},{6,2},{10,6},{... | collective-permute-start | bytes 3932168 | tf_op jit(solution)/shard_map/ppermute | solution.py:81
  38.4 0.3 fusion.23
  38.8 1.4 fusion.17
  40.2 3.8 %collective-permute-start.7 = (bf16[4,160,1024]{2,1,0:T(8,128)(2,1)}, bf16[4,160,1024]{2,1,0:T(8,128)(2,1)}, u32[]{:S(2)}, u32[]{:S(2)}) collective-permute-start(bf16[4,160,1024]{2,1,0:T(8,128)(2,1)} %fusion.17), channel_id=1, source_target_pairs={{4,0},{8,4},{12,8},{0,12},{5,1},{9,5},{13,9},{1,13},{6,2},{10,6},{... | collective-permute-start | bytes 3932168 | tf_op jit(solution)/shard_map/ppermute | solution.py:81
  44.0 1.4 fusion.19
  45.4 0.4 collective-permute-start.6
  45.8 0.1 slice_reduce_fusion
  45.9 5.5 %fusion.14 = f32[320,8]{0,1:T(8,128)S(1)} fusion(bf16[320,8,1024]{2,1,0:T(8,128)(2,1)S(1)} %bitcast.92), kind=kLoop, calls=%fused_computation.25 | loop fusion | flops 7861760 | bytes 5253120 | tf_op jit(solution)/shard_map/reduce_sum | solution.py:17
  51.4 6.5 %fusion.15 = bf16[320,8,1024]{2,0,1:T(8,128)(2,1)} fusion(f32[320,8]{0,1:T(8,128)S(1)} %add_rsqrt_fusion, bf16[320,8,1024]{2,1,0:T(8,128)(2,1)S(1)} %bitcast.92), kind=kLoop, calls=%fused_computation.26 | loop fusion | flops 7864320 | bytes 10496000 | tf_op jit(solution)/shard_map/convert_element_type | solution.py:18
  58.1 0.8 fusion.27
  58.9 0.1 convert_reduce_fusion
  59.0 0.6 reduce_max.18
  59.7 0.6 reduce_max.19
  60.3 10.4 %convolution_bitcast_fusion.3.anchor_ref = bf16[8,512,1024]{2,1,0:T(8,128)(2,1)} fusion(bf16[320,8,1024]{2,0,1:T(8,128)(2,1)} %fusion.15, s32[512]{0:T(512)S(1)} %copy-done.6, pred[512]{0:T(512)(128)(4,1)S(1)} %iota_compare_fusion.17), kind=kOutput, calls=%fused_computation.28 | convolution fusion | flops 2684682240 | bytes 13634048 | tf_op jit(solution)/shard_map/sc,cwf->wsf/dot_general | solution.py:215
  71.9 10.2 %convolution_bitcast_fusion.2.own_ref = bf16[8,512,1024]{2,1,0:T(8,128)(2,1)} fusion(bf16[320,8,1024]{2,0,1:T(8,128)(2,1)} %fusion.15, s32[512]{0:T(512)S(1)} %copy-done.4, pred[512]{0:T(512)(128)(4,1)S(1)} %get-tuple-element.74), kind=kOutput, calls=%fused_computation.27 | convolution fusion | flops 2684682240 | bytes 13634048 | tf_op jit(solution)/shard_map/sc,cwf->wsf/dot_general | solution.py:215
  82.1 11.7 %collective-permute-done.5.af_ref = bf16[4,160,1024]{2,1,0:T(8,128)(2,1)} collective-permute-done((bf16[4,160,1024]{2,1,0:T(8,128)(2,1)S(1)}, bf16[4,160,1024]{2,1,0:T(8,128)(2,1)}, u32[]{:S(2)}, u32[]{:S(2)}) %collective-permute-start.5) | collective-permute-done | bytes 1310752 | tf_op jit(solution)/shard_map/ppermute | solution.py:81
  93.8 4.2 %collective-permute-done.4.bf_ref = bf16[4,160,1024]{2,1,0:T(8,128)(2,1)} collective-permute-done((bf16[4,160,1024]{2,1,0:T(8,128)(2,1)S(1)}, bf16[4,160,1024]{2,1,0:T(8,128)(2,1)}, u32[]{:S(2)}, u32[]{:S(2)}) %collective-permute-start.4) | collective-permute-done | bytes 1310752 | tf_op jit(solution)/shard_map/ppermute | solution.py:81
  98.0 0.4 conditional.1
  98.0 0.1 broadcast.209
  98.3 9.8 %shard_map.86 = f32[4,512,128]{2,1,0:T(8,128)} custom-call(bf16[8,512,1024]{2,1,0:T(8,128)(2,1)} %convolution_bitcast_fusion.3.anchor_ref, bf16[8,512,1024]{2,1,0:T(8,128)(2,1)} %convolution_bitcast_fusion.2.own_ref, bf16[512,160]{1,0:T(8,128)(2,1)} %get-tuple-element.91.sbf_ref, bf16[512,160]{1,0:T(8,128)(2,1)} %get-tuple-element.92.saf_ref, ...), custom_call_target="tpu_custom_call" | custom-call | tf_op jit(solution)/shard_map/pallas_call | solution.py:153
  108.2 15.8 %collective-permute-done.7.af_ref = bf16[4,160,1024]{2,1,0:T(8,128)(2,1)} collective-permute-done((bf16[4,160,1024]{2,1,0:T(8,128)(2,1)}, bf16[4,160,1024]{2,1,0:T(8,128)(2,1)}, u32[]{:S(2)}, u32[]{:S(2)}) %collective-permute-start.7) | collective-permute-done | bytes 1310752 | tf_op jit(solution)/shard_map/ppermute | solution.py:81
  124.0 27.5 %collective-permute-done.6.bf_ref = bf16[4,160,1024]{2,1,0:T(8,128)(2,1)} collective-permute-done((bf16[4,160,1024]{2,1,0:T(8,128)(2,1)}, bf16[4,160,1024]{2,1,0:T(8,128)(2,1)}, u32[]{:S(2)}, u32[]{:S(2)}) %collective-permute-start.6) | collective-permute-done | bytes 1310752 | tf_op jit(solution)/shard_map/ppermute | solution.py:81
  151.5 9.9 %shard_map.87 = f32[4,512,128]{2,1,0:T(8,128)} custom-call(bf16[8,512,1024]{2,1,0:T(8,128)(2,1)} %convolution_bitcast_fusion.3.anchor_ref, bf16[8,512,1024]{2,1,0:T(8,128)(2,1)} %convolution_bitcast_fusion.2.own_ref, bf16[512,160]{1,0:T(8,128)(2,1)} %get-tuple-element.91.sbf_ref, bf16[512,160]{1,0:T(8,128)(2,1)} %get-tuple-element.92.saf_ref, ...), custom_call_target="tpu_custom_call" | custom-call | tf_op jit(solution)/shard_map/pallas_call | solution.py:153
  161.4 1.5 fusion.85
  163.0 1.5 collective-permute-done.8
  164.5 1.6 collective-permute-start.9
  166.1 0.2 select_reduce_fusion.2
  166.3 6.7 %collective-permute-done.9 = f32[512,128]{1,0:T(8,128)S(1)} collective-permute-done((f32[512,128]{1,0:T(8,128)S(1)}, f32[512,128]{1,0:T(8,128)S(1)}, u32[]{:S(2)}, u32[]{:S(2)}) %collective-permute-start.9) | collective-permute-done | bytes 262176 | tf_op jit(solution)/shard_map/ppermute | solution.py:72
  173.0 0.1 multiply_reduce_fusion.3
  173.1 1.2 multiply_reduce_fusion.2
  174.4 0.7 multiply_reduce_fusion
  175.2 1.5 collective-permute-done.10
  176.8 1.6 collective-permute-start.11
  178.3 1.2 collective-permute-done.12
  179.5 0.5 collective-permute-start.13
  180.0 5.2 %collective-permute-done.13 = f32[512]{0:T(512)S(1)} collective-permute-done((f32[512]{0:T(512)S(1)}, f32[512]{0:T(512)S(1)}, u32[]{:S(2)}, u32[]{:S(2)}) %collective-permute-start.13) | collective-permute-done | bytes 2080 | tf_op jit(solution)/shard_map/ppermute | solution.py:72
  185.2 1.0 divide_select_fusion
  (67 shorter events, 1.4 us)
Async XLA Ops:
  2.0 15.5 %collective-permute-start.2 = (s32[1,1025]{1,0:T(1,128)S(1)}, s32[1,1025]{1,0:T(1,128)S(1)}, u32[]{:S(2)}, u32[]{:S(2)}) collective-permute-start(s32[1,1025]{1,0:T(1,128)S(1)} %broadcast_in_dim.41), channel_id=1, source_target_pairs={{0,4},{4,0},{8,12},{12,8},{1,5},{5,1},{9,13},{13,9},{2,6},{6,2},{1... | collective-permute-start | bytes 12308 | tf_op jit(solution)/shard_map/ppermute | solution.py:93
  5.1 8.2 %copy-start.5 = (s32[512]{0:T(512)S(1)}, s32[512]{0:T(512)}, u32[]{:S(2)}) copy-start(s32[512]{0:T(512)} %param.11) | copy-start | bytes 6148
  5.1 8.2 %copy-start.4 = (s32[512]{0:T(512)S(1)}, s32[512]{0:T(512)}, u32[]{:S(2)}) copy-start(s32[512]{0:T(512)} %param.12) | copy-start | bytes 6148
  17.5 4.6 %collective-permute-start.3 = (s32[2,1025]{1,0:T(2,128)S(1)}, s32[2,1025]{1,0:T(2,128)S(1)}, u32[]{:S(2)}, u32[]{:S(2)}) collective-permute-start(s32[2,1025]{1,0:T(2,128)S(1)} %add_select_fusion.1), channel_id=1, source_target_pairs={{0,8},{4,12},{8,0},{12,4},{1,9},{5,13},{9,1},{13,5},{2,10},{6,14},... | collective-permute-start | bytes 24608 | tf_op jit(solution)/shard_map/ppermute | solution.py:93
  25.9 3.8 %copy-start.3 = (bf16[320,4,1024]{2,1,0:T(4,128)(2,1)S(1)}, bf16[320,4,1024]{2,1,0:T(4,128)(2,1)}, u32[]{:S(2)}) copy-start(bf16[320,4,1024]{2,1,0:T(4,128)(2,1)} %get-tuple-element.64) | copy-start | bytes 7864324
  33.6 12.3 %slice-start = ((s8[5242880]{0:T(1024)(128)(4,1)}), s8[4194304]{0:T(1024)(128)(4,1)S(1)}, s32[]{:S(2)}) async-start(s8[5242880]{0:T(1024)(128)(4,1)} %bitcast.91), calls=%async_computation | async-start | bytes 8388608
  35.6 10.3 %slice-start.1 = ((s8[5242880]{0:T(1024)(128)(4,1)}), s8[1048576]{0:T(1024)(128)(4,1)S(1)}, s32[]{:S(2)}) async-start(s8[5242880]{0:T(1024)(128)(4,1)} %bitcast.91), calls=%async_computation.1 | async-start | bytes 2097152
  35.9 57.9 %collective-permute-start.5 = (bf16[4,160,1024]{2,1,0:T(8,128)(2,1)S(1)}, bf16[4,160,1024]{2,1,0:T(8,128)(2,1)}, u32[]{:S(2)}, u32[]{:S(2)}) collective-permute-start(bf16[4,160,1024]{2,1,0:T(8,128)(2,1)S(1)} %fusion.21), channel_id=1, source_target_pairs={{4,0},{8,4},{12,8},{0,12},{5,1},{9,5},{13,9},{1,13},{6,2},{10,6},{... | collective-permute-start | bytes 3932168 | tf_op jit(solution)/shard_map/ppermute | solution.py:81
  38.7 59.2 %collective-permute-start.4 = (bf16[4,160,1024]{2,1,0:T(8,128)(2,1)S(1)}, bf16[4,160,1024]{2,1,0:T(8,128)(2,1)}, u32[]{:S(2)}, u32[]{:S(2)}) collective-permute-start(bf16[4,160,1024]{2,1,0:T(8,128)(2,1)S(1)} %fusion.23), channel_id=1, source_target_pairs={{0,4},{4,8},{8,12},{12,0},{1,5},{5,9},{9,13},{13,1},{2,6},{6,10},{... | collective-permute-start | bytes 3932168 | tf_op jit(solution)/shard_map/ppermute | solution.py:81
  40.2 83.8 %collective-permute-start.7 = (bf16[4,160,1024]{2,1,0:T(8,128)(2,1)}, bf16[4,160,1024]{2,1,0:T(8,128)(2,1)}, u32[]{:S(2)}, u32[]{:S(2)}) collective-permute-start(bf16[4,160,1024]{2,1,0:T(8,128)(2,1)} %fusion.17), channel_id=1, source_target_pairs={{4,0},{8,4},{12,8},{0,12},{5,1},{9,5},{13,9},{1,13},{6,2},{10,6},{... | collective-permute-start | bytes 3932168 | tf_op jit(solution)/shard_map/ppermute | solution.py:81
  45.4 106.1 %collective-permute-start.6 = (bf16[4,160,1024]{2,1,0:T(8,128)(2,1)}, bf16[4,160,1024]{2,1,0:T(8,128)(2,1)}, u32[]{:S(2)}, u32[]{:S(2)}) collective-permute-start(bf16[4,160,1024]{2,1,0:T(8,128)(2,1)} %fusion.19), channel_id=1, source_target_pairs={{0,4},{4,8},{8,12},{12,0},{1,5},{5,9},{9,13},{13,1},{2,6},{6,10},{... | collective-permute-start | bytes 3932168 | tf_op jit(solution)/shard_map/ppermute | solution.py:81
  51.4 8.9 %copy-start.6 = (s32[512]{0:T(512)S(1)}, s32[512]{0:T(512)}, u32[]{:S(2)}) copy-start(s32[512]{0:T(512)} %param.10) | copy-start | bytes 6148
  108.2 53.2 %copy-start.1 = (f32[4,512,128]{2,1,0:T(8,128)S(1)}, f32[4,512,128]{2,1,0:T(8,128)}, u32[]{:S(2)}) copy-start(f32[4,512,128]{2,1,0:T(8,128)} %shard_map.86) | copy-start | bytes 3145732
  161.4 4.7 %copy-start.7 = (f32[8]{0:T(128)S(1)}, f32[8]{0:T(128)}, u32[]{:S(2)}) copy-start(f32[8]{0:T(128)} %param.15) | copy-start | bytes 100
  161.4 4.7 %copy-start.8 = (s32[8]{0:T(128)S(1)}, s32[8]{0:T(128)}, u32[]{:S(2)}) copy-start(s32[8]{0:T(128)} %param.14) | copy-start | bytes 100
  162.9 1.6 collective-permute-start.8
  164.5 8.4 %collective-permute-start.9 = (f32[512,128]{1,0:T(8,128)S(1)}, f32[512,128]{1,0:T(8,128)S(1)}, u32[]{:S(2)}, u32[]{:S(2)}) collective-permute-start(f32[512,128]{1,0:T(8,128)S(1)} %add.126), channel_id=1, source_target_pairs={{0,2},{1,3},{2,0},{3,1},{4,6},{5,7},{6,4},{7,5},{8,10},{9,11},{10,... | collective-permute-start | bytes 786440 | tf_op jit(solution)/shard_map/ppermute | solution.py:72
  175.1 1.6 collective-permute-start.10
  176.8 8.5 %collective-permute-start.11 = (f32[512,128]{1,0:T(8,128)S(1)}, f32[512,128]{1,0:T(8,128)S(1)}, u32[]{:S(2)}, u32[]{:S(2)}) collective-permute-start(f32[512,128]{1,0:T(8,128)S(1)} %add.132), channel_id=1, source_target_pairs={{0,2},{1,3},{2,0},{3,1},{4,6},{5,7},{6,4},{7,5},{8,10},{9,11},{10,... | collective-permute-start | bytes 786440 | tf_op jit(solution)/shard_map/ppermute | solution.py:72
  178.3 1.2 collective-permute-start.12
  179.5 5.7 %collective-permute-start.13 = (f32[512]{0:T(512)S(1)}, f32[512]{0:T(512)S(1)}, u32[]{:S(2)}, u32[]{:S(2)}) collective-permute-start(f32[512]{0:T(512)S(1)} %add.134), channel_id=1, source_target_pairs={{0,2},{1,3},{2,0},{3,1},{4,6},{5,7},{6,4},{7,5},{8,10},{9,11},{10,... | collective-permute-start | bytes 6152 | tf_op jit(solution)/shard_map/ppermute | solution.py:72
